TPU v7x, 256 devices: a whole 4x4x8 slice. The times are simulated.
256 devices in a mesh: pipe: 2 (over core), seq: 4 (over x), tensor: 32 (over z, y).
Axes of the slice: x: 4, y: 4, z: 8, core: 2. Of those that a mesh axis runs over, the one named last changes fastest.
Arguments:
- token_ids: int32 [2, 768], P(None, 'seq'), may hold values from 0 to 511
- embed_table: bfloat16 [512, 8192], P(None, 'tensor'), may hold values from -24 to 24
- in_proj: bfloat16 [2, 8192, 3, 4096], P('pipe', None, None, 'tensor'), may hold values from -0.0625 to 0.0625
- feat_taps: float32 [2, 3, 3, 4096], P('pipe', None, None, 'tensor'), may hold values from -3 to 3
- se_taps: float32 [7, 4096], P(None, 'tensor'), may hold values from -2 to 2
- mr_taps: float32 [128, 4096], P(None, 'tensor'), may hold values from -0.6 to 0.6
- out_proj: bfloat16 [2, 4096, 8192], P('pipe', 'tensor'), may hold values from -0.1875 to 0.1875
- norm_gain: bfloat16 [2, 8192], P('pipe', 'tensor'), may hold values from 0.25 to 1.75
Outputs:
- segment_out: bfloat16 [2, 2, 768, 8192], P('pipe', None, 'seq', 'tensor')
All inputs are finite; a program needn't handle non-finite values.
Results may differ from a plain program's by a relative error of at most 0.023.
Values may be sent and summed in bfloat16 or wider, within the bound.
No kernel may reach another device: no remote copies, remote signals or barrier semaphores. Data moves between devices by JAX's collectives and lax.ppermute only.
A program may use at most 64 MiB of HBM per device.

v0:
```python
import jax
import jax.numpy as jnp
from jax import lax
from jax.sharding import PartitionSpec as P

VOCAB = 512
KL = 128
KS = 7
KF = 3
HALO = KL + KF - 2
epsilon = 1e-06


def swapped(value):
    return lax.ppermute(value, "pipe", [(0, 1), (1, 0)])


def of_section(core, own, other, section):
    return jnp.where(core == section, own, other)


def relaid_out_proj(w_down):
    n_t = lax.axis_size("tensor")
    chan_local, width = w_down.shape
    blocks = w_down.reshape(chan_local, n_t, width // n_t)
    moved = lax.all_to_all(blocks, "tensor", 1, 0, tiled=True)
    return moved.reshape(n_t * chan_local, width // n_t)


def section_step(x_in, w_in, feat, long_taps, w_out, gain):
    rows = x_in.shape[0]
    chan_local = w_in.shape[1] // 3
    aug = jnp.concatenate([x_in, gain.reshape(1, -1).astype(x_in.dtype)], axis=0)
    full = lax.all_gather(aug, "tensor", axis=1, tiled=True)
    values = full[:rows].astype(jnp.float32)
    gain_all = full[rows].astype(jnp.float32)
    inv_rms = lax.rsqrt(jnp.mean(values * values, axis=1, keepdims=True) + epsilon)
    normed = (values * inv_rms * gain_all[None, :]).astype(jnp.bfloat16)
    projected = jnp.dot(normed, w_in, preferred_element_type=jnp.float32).astype(jnp.bfloat16)
    blocks = lax.axis_size("pipe") * lax.axis_size("seq")
    kv_tail = projected[rows - HALO :, chan_local:]
    q_tail = projected[rows - (KF - 1) :, :chan_local]
    kv_prev, q_prev = lax.ppermute(
        (kv_tail, q_tail), ("pipe", "seq"), [(b, b + 1) for b in range(blocks - 1)]
    )
    q_all = jnp.concatenate([q_prev, projected[:, :chan_local]], axis=0).astype(jnp.float32)
    kv_all = jnp.concatenate([kv_prev, projected[:, chan_local:]], axis=0).astype(jnp.float32)
    q_taps = feat[:, 0, :]
    kv_taps = feat[:, 1:, :].reshape(KF, 2 * chan_local)
    kv_span = KL - 1 + rows
    q_feat = jnp.zeros((rows, chan_local), jnp.float32)
    kv_feat = jnp.zeros((kv_span, 2 * chan_local), jnp.float32)
    for tap_index in range(KF):
        offset = KF - 1 - tap_index
        q_feat = q_feat + q_taps[tap_index] * q_all[offset : offset + rows]
        kv_feat = kv_feat + kv_taps[tap_index] * kv_all[offset : offset + kv_span]
    gated_kv = kv_feat[:, :chan_local] * kv_feat[:, chan_local:]

    def add_tap(tap_index, running):
        shifted = lax.dynamic_slice_in_dim(gated_kv, KL - 1 - tap_index, rows, 0)
        return running + long_taps[tap_index] * shifted

    filtered = lax.fori_loop(0, KL, add_tap, jnp.zeros_like(q_feat))
    y_out = (q_feat * filtered).astype(jnp.bfloat16)
    y_full = lax.all_gather(y_out, "tensor", axis=1, tiled=True)
    mixed = jnp.dot(y_full, w_out, preferred_element_type=jnp.float32)
    return (x_in.astype(jnp.float32) + mixed).astype(jnp.bfloat16)


def local(token_ids, embed_table, in_proj, feat_taps, se_taps, mr_taps, out_proj, norm_gain):
    core = lax.axis_index("pipe")
    w_own = in_proj[0].reshape(in_proj.shape[1], -1)
    feat_own = feat_taps[0]
    gain_own = norm_gain[0]
    wt_own = relaid_out_proj(out_proj[0])
    w_other, feat_other, gain_other, wt_other = swapped((w_own, feat_own, gain_own, wt_own))
    padded_se = jnp.concatenate(
        [se_taps, jnp.zeros((KL - KS, se_taps.shape[1]), jnp.float32)], axis=0
    )
    filters = (padded_se, mr_taps)
    ids = lax.dynamic_index_in_dim(token_ids, core, 0, keepdims=False)
    vocab_ids = jnp.arange(VOCAB, dtype=jnp.int32)
    one_hot = (ids[:, None] == vocab_ids[None, :]).astype(jnp.bfloat16)
    current = jnp.dot(one_hot, embed_table, preferred_element_type=jnp.float32).astype(jnp.bfloat16)
    results = []
    for section in range(2):
        current = section_step(
            current,
            of_section(core, w_own, w_other, section),
            of_section(core, feat_own, feat_other, section),
            filters[section],
            of_section(core, wt_own, wt_other, section),
            of_section(core, gain_own, gain_other, section),
        )
        results.append(current)
    first_mine, second_mine = results
    second_slice_of_first = lax.ppermute(first_mine, "pipe", [(1, 0)])
    first_slice_of_second = lax.ppermute(second_mine, "pipe", [(0, 1)])
    lead = core == 0
    slice_zero = jnp.where(lead, first_mine, first_slice_of_second)
    slice_one = jnp.where(lead, second_slice_of_first, second_mine)
    return jnp.stack([slice_zero, slice_one], axis=0)[None]


def solution(mesh):
    return jax.shard_map(
        local,
        mesh=mesh,
        in_specs=(
            P(None, "seq"),
            P(None, "tensor"),
            P("pipe", None, None, "tensor"),
            P("pipe", None, None, "tensor"),
            P(None, "tensor"),
            P(None, "tensor"),
            P("pipe", "tensor", None),
            P("pipe", "tensor"),
        ),
        out_specs=P("pipe", None, "seq", "tensor"),
        check_vma=False,
    )
```

profile of v0, /device:TPU:1, one launch (start us, length us, event | category | flops | bytes accessed | tf_op | source)
XLA Modules:
  0.0 497.7 jit_solution(15193292453883227668)
XLA Ops:
  6.5 0.7 reduce
  7.3 3.3 collective-permute-start.1
  12.3 8.9 %copy.10 = bf16[1,8192,3,128]{1,3,2,0:T(8,128)(2,1)} copy(bf16[1,8192,3,128]{3,1,2,0:T(8,128)(2,1)} %param.14) | data formatting | bytes 12582912 | tf_op args[2]
  21.7 2.4 copy.11
  24.1 9.5 %all-to-all-start = ((bf16[128,32,256]{0,2,1:T(8,128)(2,1)}), bf16[128,32,256]{0,2,1:T(8,128)(2,1)S(1)}, u32[]{:S(2)}, u32[]{:S(2)}) async-start(bf16[128,32,256]{0,2,1:T(8,128)(2,1)} %bitcast.58), calls=%async_computation | async-start | bytes 4194304 | tf_op jit(solution)/shard_map/all_to_all | solution.py:26
  33.7 75.9 %all-gather.5.cloned.1.call-done = bf16[193,8192]{1,0:T(8,128)(2,1)} async-done(((bf16[193,256]{1,0:T(8,128)(2,1)}), bf16[193,8192]{1,0:T(8,128)(2,1)}) %all-gather.5.cloned.1.call-update) | async-done | bytes 3162128 | tf_op jit(solution)/shard_map/all_gather | solution.py:34
  109.6 2.6 fusion
  112.2 0.9 slice_convert_fusion.1
  113.1 6.0 %fusion.26 = bf16[192,384]{1,0:T(8,128)(2,1)S(1)} fusion(bf16[8192,384]{0,1:T(8,128)(2,1)} %bitcast.60, bf16[8192,384]{0,1:T(8,128)(2,1)} %collective-permute-done.2, pred[]{:T(512)S(6)} %eq.12, f32[8192]{0:T(1024)S(1)} %bitcast.65, f32[192]{0:T(256)S(1)} %add_rsqrt_fusion.1, bf16[193,8192]{1,0:T(8,128)(2,1)} %all-gather.5.cloned.1.call-done), kind=kOutput, calls=%fused_computation.32 | convolution fusion | flops 1217470464 | bytes 15909633 | tf_op jit(solution)/shard_map/dot_general | solution.py:39
  119.1 3.1 collective-permute-start.3
  122.3 3.0 collective-permute-start.4
  125.3 2.7 collective-permute-done.3
  128.1 2.7 collective-permute-done.4
  131.0 10.6 %while.32 = (s32[]{:T(128)}, f32[192,128]{1,0:T(8,128)S(1)}, f32[128,128]{1,0:T(8,128)S(1)}, f32[319,128]{1,0:T(8,128)S(1)}, s32[]{:T(128)}, /*index=5*/s32[]{:T(128)}, s32[]{:T(128)}, s32[]{:T(128)}) while((s32[]{:T(128)}, f32[192,128]{1,0:T(8,128)S(1)}, f32[128,128]{1,0:T(8,128)S(1)}, f32[319,128]{1,0:T(8,128)S(1)}, s32[]{:T(128)}, ...), condition=%wide.region_2.3_spmd.clone, body=%wide.region_1.2_spmd.clone.sunk | while | flops 73735 | bytes 296597 | solution.py:63
  142.4 2.9 copy.12
  145.8 4.0 collective-permute-done.5
  149.8 60.7 %all-gather.7.cloned.1.call-done = bf16[192,4096]{1,0:T(8,128)(2,1)} async-done(((bf16[192,128]{1,0:T(8,128)(2,1)}), bf16[192,4096]{1,0:T(8,128)(2,1)}) %all-gather.7.cloned.1.call-update) | async-done | bytes 1572880 | tf_op jit(solution)/shard_map/all_gather | solution.py:65
  210.5 2.0 fusion.39
  213.3 80.0 %all-gather.9.cloned.1.call-done = bf16[193,8192]{1,0:T(8,128)(2,1)} async-done(((bf16[193,256]{1,0:T(8,128)(2,1)}), bf16[193,8192]{1,0:T(8,128)(2,1)}) %all-gather.9.cloned.1.call-update) | async-done | bytes 3162128 | tf_op jit(solution)/shard_map/all_gather | solution.py:34
  293.3 2.6 fusion.3
  295.9 0.9 slice_convert_fusion
  296.8 6.0 %fusion.31 = bf16[192,384]{1,0:T(8,128)(2,1)S(1)} fusion(bf16[8192,384]{0,1:T(8,128)(2,1)} %bitcast.61, bf16[8192,384]{0,1:T(8,128)(2,1)} %collective-permute-done.2, pred[]{:T(512)S(6)} %eq.33, f32[8192]{0:T(1024)S(1)} %bitcast.66, f32[192]{0:T(256)S(1)} %add_rsqrt_fusion, bf16[193,8192]{1,0:T(8,128)(2,1)} %all-gather.9.cloned.1.call-done), kind=kOutput, calls=%fused_computation.33 | convolution fusion | flops 1217470464 | bytes 15909633 | tf_op jit(solution)/shard_map/dot_general | solution.py:39
  302.8 3.2 collective-permute-start.6
  306.1 3.1 collective-permute-start.7
  309.2 2.2 collective-permute-done.6
  311.5 2.7 collective-permute-done.7
  314.4 96.0 %while.33 = (s32[]{:T(128)}, f32[192,128]{1,0:T(8,128)S(1)}, f32[128,128]{1,0:T(8,128)}, f32[319,128]{1,0:T(8,128)S(1)}, s32[]{:T(128)}, /*index=5*/s32[]{:T(128)}, s32[]{:T(128)}, s32[]{:T(128)}) while((s32[]{:T(128)}, f32[192,128]{1,0:T(8,128)S(1)}, f32[128,128]{1,0:T(8,128)}, f32[319,128]{1,0:T(8,128)S(1)}, s32[]{:T(128)}, ...), condition=%wide.region_5.6_spmd.clone, body=%wide.region_4.5_spmd.clone.sunk | while | flops 73735 | bytes 296597 | solution.py:63
  411.1 2.5 collective-permute-start.9
  413.6 68.0 %all-gather.11.cloned.1.call-done = bf16[192,4096]{1,0:T(8,128)(2,1)} async-done(((bf16[192,128]{1,0:T(8,128)(2,1)}), bf16[192,4096]{1,0:T(8,128)(2,1)}) %all-gather.11.cloned.1.call-update) | async-done | bytes 1572880 | tf_op jit(solution)/shard_map/all_gather | solution.py:65
  481.6 2.0 fusion.20
  483.7 1.3 collective-permute-start.8
  485.0 5.4 %collective-permute-done.8 = bf16[192,256]{1,0:T(8,128)(2,1)S(1)} collective-permute-done((bf16[192,256]{1,0:T(8,128)(2,1)S(1)}, bf16[192,256]{1,0:T(8,128)(2,1)S(1)}, u32[]{:S(2)}, u32[]{:S(2)}) %collective-permute-start.8) | collective-permute-done | bytes 98336 | tf_op jit(solution)/shard_map/ppermute | solution.py:98
  (579 shorter events, 104.6 us)
Async XLA Ops:
  6.5 4.7 copy-start
  6.5 103.0 %all-gather.5.cloned.1.call-start = ((), (), s32[]{:S(2)}) async-start(), calls=%async_computation.1 | async-start | bytes 3379200 | tf_op jit(solution)/shard_map/all_gather | solution.py:34
  7.3 4.3 collective-permute-start.1
  12.3 9.0 %copy-start.3 = (f32[1,3,3,128]{3,0,2,1:T(1,128)S(1)}, f32[1,3,3,128]{3,0,2,1:T(1,128)}, u32[]{:S(2)}) copy-start(f32[1,3,3,128]{3,0,2,1:T(1,128)} %param.15) | copy-start | bytes 13828
  12.3 9.4 %copy-start.1 = (bf16[1,128,8192]{2,1,0:T(8,128)(2,1)S(1)}, bf16[1,128,8192]{2,1,0:T(8,128)(2,1)}, u32[]{:S(2)}) copy-start(bf16[1,128,8192]{2,1,0:T(8,128)(2,1)} %param.18) | copy-start | bytes 6291460
  21.1 92.0 %collective-permute-start.2 = (bf16[8192,384]{0,1:T(8,128)(2,1)}, bf16[8192,384]{0,1:T(8,128)(2,1)}, u32[]{:S(2)}, u32[]{:S(2)}) collective-permute-start(bf16[8192,384]{0,1:T(8,128)(2,1)} %bitcast.59), channel_id=1, source_target_pairs={{0,128},{128,0},{1,129},{129,1},{2,130},{130,2},{3,131},{131,3},{4... | collective-permute-start | bytes 18874376 | tf_op jit(solution)/shard_map/ppermute | solution.py:15
  21.3 12.4 %copy-start.4 = (f32[7,128]{1,0:T(8,128)S(1)}, f32[7,128]{1,0:T(8,128)}, u32[]{:S(2)}) copy-start(f32[7,128]{1,0:T(8,128)} %param.16) | copy-start | bytes 10756
  21.3 12.4 %collective-permute-start = (f32[3,3,128]{2,1,0:T(4,128)S(1)}, f32[3,3,128]{2,1,0:T(4,128)S(1)}, u32[]{:S(2)}, u32[]{:S(2)}) collective-permute-start(f32[3,3,128]{2,1,0:T(4,128)S(1)} %bitcast.67), channel_id=1, source_target_pairs={{0,128},{128,0},{1,129},{129,1},{2,130},{130,2},{3,131},{131,3},{4... | collective-permute-start | bytes 13832 | tf_op jit(solution)/shard_map/ppermute | solution.py:15
  24.1 118.2 %all-to-all-start = ((bf16[128,32,256]{0,2,1:T(8,128)(2,1)}), bf16[128,32,256]{0,2,1:T(8,128)(2,1)S(1)}, u32[]{:S(2)}, u32[]{:S(2)}) async-start(bf16[128,32,256]{0,2,1:T(8,128)(2,1)} %bitcast.58), calls=%async_computation | async-start | bytes 4194304 | tf_op jit(solution)/shard_map/all_to_all | solution.py:26
  33.6 176.9 %all-gather.7.cloned.1.call-start = ((), (), s32[]{:S(2)}) async-start(), calls=%async_computation.2 | async-start | bytes 1622016 | tf_op jit(solution)/shard_map/all_gather | solution.py:65
  119.1 8.9 %collective-permute-start.3 = (bf16[2,128]{1,0:T(2,128)(2,1)S(1)}, bf16[2,128]{1,0:T(2,128)(2,1)S(1)}, u32[]{:S(2)}, u32[]{:S(2)}) collective-permute-start(bf16[2,128]{1,0:T(2,128)(2,1)S(1)} %slice.191), channel_id=1, source_target_pairs={{0,32},{32,64},{64,96},{96,128},{128,160},{160,192},{192,224},{1,3... | collective-permute-start | bytes 1544 | tf_op jit(solution)/shard_map/ppermute | solution.py:43
  122.3 8.5 %collective-permute-start.4 = (bf16[129,256]{1,0:T(8,128)(2,1)S(1)}, bf16[129,256]{1,0:T(8,128)(2,1)S(1)}, u32[]{:S(2)}, u32[]{:S(2)}) collective-permute-start(bf16[129,256]{1,0:T(8,128)(2,1)S(1)} %slice.199), channel_id=1, source_target_pairs={{0,32},{32,64},{64,96},{96,128},{128,160},{160,192},{192,224},{1,3... | collective-permute-start | bytes 198152 | tf_op jit(solution)/shard_map/ppermute | solution.py:43
  142.3 151.0 %all-gather.9.cloned.1.call-start = ((), (), s32[]{:S(2)}) async-start(), calls=%async_computation.3 | async-start | bytes 3379200 | tf_op jit(solution)/shard_map/all_gather | solution.py:34
  145.3 4.5 collective-permute-start.5
  149.8 62.7 %copy-start.5 = (bf16[4096,256]{1,0:T(8,128)(2,1)}, bf16[4096,256]{1,0:T(8,128)(2,1)S(1)}, u32[]{:S(2)}) copy-start(bf16[4096,256]{1,0:T(8,128)(2,1)S(1)} %collective-permute-done.5) | copy-start | bytes 6291460
  213.2 268.4 %all-gather.11.cloned.1.call-start = ((), (), s32[]{:S(2)}) async-start(), calls=%async_computation.4 | async-start | bytes 1622016 | tf_op jit(solution)/shard_map/all_gather | solution.py:65
  302.8 178.8 %copy-start.2 = (bf16[32,128,1,256]{3,1,0,2:T(8,128)(2,1)S(1)}, bf16[32,128,1,256]{3,1,0,2:T(8,128)(2,1)}, u32[]{:S(2)}) copy-start(bf16[32,128,1,256]{3,1,0,2:T(8,128)(2,1)} %copy.12) | copy-start | bytes 6291460
  302.8 8.6 %collective-permute-start.6 = (bf16[2,128]{1,0:T(2,128)(2,1)S(1)}, bf16[2,128]{1,0:T(2,128)(2,1)S(1)}, u32[]{:S(2)}, u32[]{:S(2)}) collective-permute-start(bf16[2,128]{1,0:T(2,128)(2,1)S(1)} %slice.211), channel_id=1, source_target_pairs={{0,32},{32,64},{64,96},{96,128},{128,160},{160,192},{192,224},{1,3... | collective-permute-start | bytes 1544 | tf_op jit(solution)/shard_map/ppermute | solution.py:43
  306.1 8.1 %collective-permute-start.7 = (bf16[129,256]{1,0:T(8,128)(2,1)S(1)}, bf16[129,256]{1,0:T(8,128)(2,1)S(1)}, u32[]{:S(2)}, u32[]{:S(2)}) collective-permute-start(bf16[129,256]{1,0:T(8,128)(2,1)S(1)} %slice.219), channel_id=1, source_target_pairs={{0,32},{32,64},{64,96},{96,128},{128,160},{160,192},{192,224},{1,3... | collective-permute-start | bytes 198152 | tf_op jit(solution)/shard_map/ppermute | solution.py:43
  411.1 72.6 %collective-permute-start.9 = (bf16[192,256]{1,0:T(8,128)(2,1)S(1)}, bf16[192,256]{1,0:T(8,128)(2,1)S(1)}, u32[]{:S(2)}, u32[]{:S(2)}) collective-permute-start(bf16[192,256]{1,0:T(8,128)(2,1)S(1)} %fusion.39), channel_id=1, source_target_pairs={{128,0},{129,1},{130,2},{131,3},{132,4},{133,5},{134,6},{135,7},{1... | collective-permute-start | bytes 294920 | tf_op jit(solution)/shard_map/ppermute | solution.py:97
  483.7 6.7 %collective-permute-start.8 = (bf16[192,256]{1,0:T(8,128)(2,1)S(1)}, bf16[192,256]{1,0:T(8,128)(2,1)S(1)}, u32[]{:S(2)}, u32[]{:S(2)}) collective-permute-start(bf16[192,256]{1,0:T(8,128)(2,1)S(1)} %get-tuple-element.274), channel_id=1, source_target_pairs={{0,128},{1,129},{2,130},{3,131},{4,132},{5,133},{6,134},{7,135},{8... | collective-permute-start | bytes 294920 | tf_op jit(solution)/shard_map/ppermute | solution.py:98
Sparse Core Ops, SparseCore 0:
  12.4 97.1 all-gather.4
  142.4 68.0 all-gather.6
  213.3 79.9 all-gather.8
  411.2 70.3 all-gather.10
where the time goes:
time: 502 us; the launch traced here: 498 us
  waiting for transfers between devices  305 us (61%)
  local copies, waits for them, and re-layouts  105 us (21%)
  starting transfers between devices  30.1 us (6%)
  other arithmetic  19.8 us (4%)
  matrix products  16.2 us (3%)
  between operations  13.5 us (3%)
  loops' own time  8.15 us (2%)
    all_gather x2, waiting for transfers between devices, section_step(): full = lax.all_gather(aug, 'tensor', axis=1, tiled=True)  156 us
    all_gather x2, waiting for transfers between devices, section_step(): y_full = lax.all_gather(y_out, 'tensor', axis=1, tiled=True)  129 us
    mul x256, local copies, waits for them, and re-layouts, add_tap(): return running + long_taps[tap_index] * shifted  90.3 us
    ppermute x4, starting transfers between devices, section_step(): lax.ppermute((kv_tail, q_tail), ('pipe', 'seq'), [(b, b + 1) for b in ran...  12.4 us
    dot_general x2, matrix products, section_step(): jnp.dot(normed, w_in, preferred_element_type=jnp.float32)  12 us
    unnamed x15, local copies, waits for them, and re-layouts  11.3 us
    ppermute x4, waiting for transfers between devices, section_step(): lax.ppermute((kv_tail, q_tail), ('pipe', 'seq'), [(b, b + 1) for b in ran...  10.5 us
  transfers between devices with their start and end apart: 15, of which 10 were waited for; matrix products, arithmetic and copies ran while one was open for 7% of the time, Pallas kernels for 0%

commit v1 on v0

--- a/solution.py
+++ b/solution.py
@@ -31,7 +31,9 @@
     rows = x_in.shape[0]
     chan_local = w_in.shape[1] // 3
     aug = jnp.concatenate([x_in, gain.reshape(1, -1).astype(x_in.dtype)], axis=0)
-    full = lax.all_gather(aug, "tensor", axis=1, tiled=True)
+    full = jnp.concatenate(
+        lax.all_to_all(jnp.stack([aug] * lax.axis_size("tensor")), "tensor", 0, 0), axis=1
+    )
     values = full[:rows].astype(jnp.float32)
     gain_all = full[rows].astype(jnp.float32)
     inv_rms = lax.rsqrt(jnp.mean(values * values, axis=1, keepdims=True) + epsilon)

time: 502 us -> 583 us (1.16)
  local copies, waits for them, and re-layouts: 105 us -> 202 us
  waiting for transfers between devices: 305 us -> 280 us
  starting transfers between devices: 30.1 us -> 44.8 us
  other arithmetic: 19.8 us -> 13.9 us
    all_gather x2 -> x0, waiting for transfers between devices: 156 us -> none  [section_step(): full = lax.all_gather(aug, 'tensor', axis=1, tiled=True)]
    all_to_all x0 -> x2, waiting for transfers between devices: none -> 127 us  [section_step(): lax.all_to_all(jnp.stack([aug] * lax.axis_size('tensor')), 'tensor', 0, 0)]
    mul x256, local copies, waits for them, and re-layouts: 90.3 us -> 177 us  [add_tap(): return running + long_taps[tap_index] * shifted]
    all_to_all x0 -> x2, starting transfers between devices: none -> 16.4 us  [section_step(): lax.all_to_all(jnp.stack([aug] * lax.axis_size('tensor')), 'tensor', 0, 0)]
    ppermute x4, waiting for transfers between devices: 10.5 us -> 18.2 us  [section_step(): lax.ppermute((kv_tail, q_tail), ('pipe', 'seq'), [(b, b + 1) for b in ran...]
    unnamed x15 -> x31, local copies, waits for them, and re-layouts: 11.3 us -> 15 us
  transfers between devices with their start and end apart: 15 -> 15, of which waited for: 10 -> 11; matrix products, arithmetic and copies ran while one was open for 7% -> 21% of each run, Pallas kernels for 0% -> 0%
where the time goes in v1:
time: 583 us; the launch traced here: 574 us
  waiting for transfers between devices  280 us (48%)
  local copies, waits for them, and re-layouts  202 us (35%)
  starting transfers between devices  44.8 us (8%)
  between operations  14 us (2%)
  other arithmetic  13.9 us (2%)
  matrix products  12.5 us (2%)
  loops' own time  6.6 us (1%)
    mul x256, local copies, waits for them, and re-layouts, add_tap(): return running + long_taps[tap_index] * shifted  177 us
    all_to_all x2, waiting for transfers between devices, section_step(): lax.all_to_all(jnp.stack([aug] * lax.axis_size('tensor')), 'tensor', 0, 0)  127 us
    all_gather x2, waiting for transfers between devices, section_step(): y_full = lax.all_gather(y_out, 'tensor', axis=1, tiled=True)  124 us
    ppermute x4, waiting for transfers between devices, section_step(): lax.ppermute((kv_tail, q_tail), ('pipe', 'seq'), [(b, b + 1) for b in ran...  18.2 us
    all_to_all x2, starting transfers between devices, section_step(): lax.all_to_all(jnp.stack([aug] * lax.axis_size('tensor')), 'tensor', 0, 0)  16.4 us
    unnamed x31, local copies, waits for them, and re-layouts  15 us
    ppermute x4, starting transfers between devices, section_step(): lax.ppermute((kv_tail, q_tail), ('pipe', 'seq'), [(b, b + 1) for b in ran...  12.6 us
  transfers between devices with their start and end apart: 15, of which 11 were waited for; matrix products, arithmetic and copies ran while one was open for 21% of the time, Pallas kernels for 0%

profile of v1, /device:TPU:1, one launch (start us, length us, event | category | flops | bytes accessed | tf_op | source)
XLA Modules:
  0.0 573.6 jit_solution(5851409230591181254)
XLA Ops:
  7.3 3.3 collective-permute-start.1
  11.6 1.9 stack.10
  13.5 9.5 %all-to-all-start = ((bf16[32,193,256]{2,1,0:T(8,128)(2,1)}), bf16[32,193,256]{2,1,0:T(8,128)(2,1)S(1)}, u32[]{:S(2)}, u32[]{:S(2)}) async-start(bf16[32,193,256]{2,1,0:T(8,128)(2,1)} %stack.10), calls=%async_computation | async-start | bytes 6553600 | tf_op jit(solution)/shard_map/all_to_all | solution.py:35
  23.0 8.6 %copy.14 = bf16[1,8192,3,128]{1,3,2,0:T(8,128)(2,1)} copy(bf16[1,8192,3,128]{3,1,2,0:T(8,128)(2,1)} %param.14) | data formatting | bytes 12582912 | tf_op args[2]
  32.1 4.1 copy.15
  37.1 59.6 %all-to-all-done = bf16[32,193,256]{2,1,0:T(8,128)(2,1)S(1)} async-done(((bf16[32,193,256]{2,1,0:T(8,128)(2,1)}), bf16[32,193,256]{2,1,0:T(8,128)(2,1)S(1)}, u32[]{:S(2)}, u32[]{:S(2)}) %all-to-all-start) | async-done | bytes 3162144 | tf_op jit(solution)/shard_map/all_to_all | solution.py:35
  96.7 7.7 %all-to-all-start.1 = ((bf16[128,32,256]{0,2,1:T(8,128)(2,1)}), bf16[128,32,256]{0,2,1:T(8,128)(2,1)}, u32[]{:S(2)}, u32[]{:S(2)}) async-start(bf16[128,32,256]{0,2,1:T(8,128)(2,1)} %bitcast.71), calls=%async_computation.1 | async-start | bytes 4194304 | tf_op jit(solution)/shard_map/all_to_all | solution.py:26
  105.3 0.8 copy.19
  107.6 5.2 fusion.18
  112.8 3.1 collective-permute-start.3
  116.0 3.1 collective-permute-start.4
  119.3 3.9 collective-permute-done.4
  123.4 95.2 %while.32 = (s32[]{:T(128)}, f32[192,128]{1,0:T(8,128)S(1)}, f32[128,128]{1,0:T(8,128)}, f32[319,128]{1,0:T(8,128)S(1)}, s32[]{:T(128)}, /*index=5*/s32[]{:T(128)}, s32[]{:T(128)}, s32[]{:T(128)}) while((s32[]{:T(128)}, f32[192,128]{1,0:T(8,128)S(1)}, f32[128,128]{1,0:T(8,128)}, f32[319,128]{1,0:T(8,128)S(1)}, s32[]{:T(128)}, ...), condition=%wide.region_2.3_spmd.clone, body=%wide.region_1.2_spmd.clone.sunk | while | flops 73735 | bytes 296605 | solution.py:65
  219.3 3.3 copy.16
  222.7 4.3 collective-permute-done.5
  226.9 60.2 %all-gather.3.cloned.1.call-done = bf16[192,4096]{1,0:T(8,128)(2,1)} async-done(((bf16[192,128]{1,0:T(8,128)(2,1)}), bf16[192,4096]{1,0:T(8,128)(2,1)}) %all-gather.3.cloned.1.call-update) | async-done | bytes 1572880 | tf_op jit(solution)/shard_map/all_gather | solution.py:67
  287.1 2.7 fusion.27
  289.8 1.9 stack.11
  291.7 6.9 %all-to-all-start.2 = ((bf16[32,193,256]{2,1,0:T(8,128)(2,1)}), bf16[32,193,256]{2,1,0:T(8,128)(2,1)S(1)}, u32[]{:S(2)}, u32[]{:S(2)}) async-start(bf16[32,193,256]{2,1,0:T(8,128)(2,1)} %stack.11), calls=%async_computation.2 | async-start | bytes 6553600 | tf_op jit(solution)/shard_map/all_to_all | solution.py:35
  298.9 67.5 %all-to-all-done.2 = bf16[32,193,256]{2,1,0:T(8,128)(2,1)S(1)} async-done(((bf16[32,193,256]{2,1,0:T(8,128)(2,1)}), bf16[32,193,256]{2,1,0:T(8,128)(2,1)S(1)}, u32[]{:S(2)}, u32[]{:S(2)}) %all-to-all-start.2) | async-done | bytes 3162144 | tf_op jit(solution)/shard_map/all_to_all | solution.py:35
  369.4 0.9 slice-done.3
  370.3 2.4 fusion.21
  372.7 3.2 collective-permute-start.6
  376.0 3.1 collective-permute-start.7
  379.1 11.4 %collective-permute-done.6 = bf16[2,128]{1,0:T(2,128)(2,1)S(1)} collective-permute-done((bf16[2,128]{1,0:T(2,128)(2,1)S(1)}, bf16[2,128]{1,0:T(2,128)(2,1)S(1)}, u32[]{:S(2)}, u32[]{:S(2)}) %collective-permute-start.6) | collective-permute-done | bytes 544 | tf_op jit(solution)/shard_map/ppermute | solution.py:45
  390.5 2.7 collective-permute-done.7
  393.4 96.5 %while.33 = (s32[]{:T(128)}, f32[192,128]{1,0:T(8,128)S(1)}, f32[128,128]{1,0:T(8,128)}, f32[319,128]{1,0:T(8,128)S(1)}, s32[]{:T(128)}, /*index=5*/s32[]{:T(128)}, s32[]{:T(128)}, s32[]{:T(128)}) while((s32[]{:T(128)}, f32[192,128]{1,0:T(8,128)S(1)}, f32[128,128]{1,0:T(8,128)}, f32[319,128]{1,0:T(8,128)S(1)}, s32[]{:T(128)}, ...), condition=%wide.region_5.6_spmd.clone, body=%wide.region_4.5_spmd.clone.sunk | while | flops 73735 | bytes 296605 | solution.py:65
  490.7 2.6 collective-permute-start.9
  493.3 63.9 %all-gather.5.cloned.1.call-done = bf16[192,4096]{1,0:T(8,128)(2,1)} async-done(((bf16[192,128]{1,0:T(8,128)(2,1)}), bf16[192,4096]{1,0:T(8,128)(2,1)}) %all-gather.5.cloned.1.call-update) | async-done | bytes 1572880 | tf_op jit(solution)/shard_map/all_gather | solution.py:67
  557.2 2.0 fusion.12
  559.3 1.3 collective-permute-start.8
  560.6 5.4 collective-permute-done.8
  (601 shorter events, 196.5 us)
Async XLA Ops:
  6.5 4.7 copy-start
  7.3 4.3 collective-permute-start.1
  11.5 1.9 copy-start.6
  13.5 83.3 %all-to-all-start = ((bf16[32,193,256]{2,1,0:T(8,128)(2,1)}), bf16[32,193,256]{2,1,0:T(8,128)(2,1)S(1)}, u32[]{:S(2)}, u32[]{:S(2)}) async-start(bf16[32,193,256]{2,1,0:T(8,128)(2,1)} %stack.10), calls=%async_computation | async-start | bytes 6553600 | tf_op jit(solution)/shard_map/all_to_all | solution.py:35
  23.0 9.1 %copy-start.8 = (f32[1,3,3,128]{3,0,2,1:T(1,128)S(1)}, f32[1,3,3,128]{3,0,2,1:T(1,128)}, u32[]{:S(2)}) copy-start(f32[1,3,3,128]{3,0,2,1:T(1,128)} %param.15) | copy-start | bytes 13828
  31.6 4.6 copy-start.9
  31.6 75.3 %collective-permute-start.2 = (bf16[8192,384]{0,1:T(8,128)(2,1)}, bf16[8192,384]{0,1:T(8,128)(2,1)}, u32[]{:S(2)}, u32[]{:S(2)}) collective-permute-start(bf16[8192,384]{0,1:T(8,128)(2,1)} %bitcast.72), channel_id=1, source_target_pairs={{0,128},{128,0},{1,129},{129,1},{2,130},{130,2},{3,131},{131,3},{4... | collective-permute-start | bytes 18874376 | tf_op jit(solution)/shard_map/ppermute | solution.py:15
  32.0 5.1 collective-permute-start
  96.7 122.5 %all-to-all-start.1 = ((bf16[128,32,256]{0,2,1:T(8,128)(2,1)}), bf16[128,32,256]{0,2,1:T(8,128)(2,1)}, u32[]{:S(2)}, u32[]{:S(2)}) async-start(bf16[128,32,256]{0,2,1:T(8,128)(2,1)} %bitcast.71), calls=%async_computation.1 | async-start | bytes 4194304 | tf_op jit(solution)/shard_map/all_to_all | solution.py:26
  104.5 182.7 %all-gather.3.cloned.1.call-start = ((), (), s32[]{:S(2)}) async-start(), calls=%async_computation.3 | async-start | bytes 1622016 | tf_op jit(solution)/shard_map/all_gather | solution.py:67
  104.5 2.3 slice-start
  105.3 2.3 slice-start.1
  112.8 6.5 %collective-permute-start.3 = (bf16[2,128]{1,0:T(2,128)(2,1)S(1)}, bf16[2,128]{1,0:T(2,128)(2,1)S(1)}, u32[]{:S(2)}, u32[]{:S(2)}) collective-permute-start(bf16[2,128]{1,0:T(2,128)(2,1)S(1)} %slice.195), channel_id=1, source_target_pairs={{0,32},{32,64},{64,96},{96,128},{128,160},{160,192},{192,224},{1,3... | collective-permute-start | bytes 1544 | tf_op jit(solution)/shard_map/ppermute | solution.py:45
  116.0 7.2 %collective-permute-start.4 = (bf16[129,256]{1,0:T(8,128)(2,1)S(1)}, bf16[129,256]{1,0:T(8,128)(2,1)S(1)}, u32[]{:S(2)}, u32[]{:S(2)}) collective-permute-start(bf16[129,256]{1,0:T(8,128)(2,1)S(1)} %slice.203), channel_id=1, source_target_pairs={{0,32},{32,64},{64,96},{96,128},{128,160},{160,192},{192,224},{1,3... | collective-permute-start | bytes 198152 | tf_op jit(solution)/shard_map/ppermute | solution.py:45
  123.4 163.7 %copy-start.7 = (bf16[192,256]{1,0:T(8,128)(2,1)S(1)}, bf16[192,256]{1,0:T(8,128)(2,1)}, u32[]{:S(2)}) copy-start(bf16[192,256]{1,0:T(8,128)(2,1)} %copy-done.6) | copy-start | bytes 294916
  222.6 67.3 %copy-start.2 = (bf16[32,128,1,256]{3,1,0,2:T(8,128)(2,1)}, bf16[32,128,1,256]{3,1,0,2:T(8,128)(2,1)S(1)}, u32[]{:S(2)}) copy-start(bf16[32,128,1,256]{3,1,0,2:T(8,128)(2,1)S(1)} %copy.16) | copy-start | bytes 6291460
  222.6 4.4 collective-permute-start.5
  289.8 1.9 copy-start.4
  291.7 74.7 %all-to-all-start.2 = ((bf16[32,193,256]{2,1,0:T(8,128)(2,1)}), bf16[32,193,256]{2,1,0:T(8,128)(2,1)S(1)}, u32[]{:S(2)}, u32[]{:S(2)}) async-start(bf16[32,193,256]{2,1,0:T(8,128)(2,1)} %stack.11), calls=%async_computation.2 | async-start | bytes 6553600 | tf_op jit(solution)/shard_map/all_to_all | solution.py:35
  298.7 258.6 %all-gather.5.cloned.1.call-start = ((), (), s32[]{:S(2)}) async-start(), calls=%async_computation.4 | async-start | bytes 1622016 | tf_op jit(solution)/shard_map/all_gather | solution.py:67
  367.2 2.2 slice-start.2
  368.0 2.3 slice-start.3
  372.7 118.0 %copy-start.5 = (bf16[192,256]{1,0:T(8,128)(2,1)S(1)}, bf16[192,256]{1,0:T(8,128)(2,1)}, u32[]{:S(2)}) copy-start(bf16[192,256]{1,0:T(8,128)(2,1)} %copy-done.4) | copy-start | bytes 294916
  372.7 184.6 %copy-start.3 = (bf16[32,128,1,256]{3,1,0,2:T(8,128)(2,1)S(1)}, bf16[32,128,1,256]{3,1,0,2:T(8,128)(2,1)}, u32[]{:S(2)}) copy-start(bf16[32,128,1,256]{3,1,0,2:T(8,128)(2,1)} %copy-done.2) | copy-start | bytes 6291460
  372.7 17.8 %collective-permute-start.6 = (bf16[2,128]{1,0:T(2,128)(2,1)S(1)}, bf16[2,128]{1,0:T(2,128)(2,1)S(1)}, u32[]{:S(2)}, u32[]{:S(2)}) collective-permute-start(bf16[2,128]{1,0:T(2,128)(2,1)S(1)} %slice.215), channel_id=1, source_target_pairs={{0,32},{32,64},{64,96},{96,128},{128,160},{160,192},{192,224},{1,3... | collective-permute-start | bytes 1544 | tf_op jit(solution)/shard_map/ppermute | solution.py:45
  376.0 17.2 %collective-permute-start.7 = (bf16[129,256]{1,0:T(8,128)(2,1)S(1)}, bf16[129,256]{1,0:T(8,128)(2,1)S(1)}, u32[]{:S(2)}, u32[]{:S(2)}) collective-permute-start(bf16[129,256]{1,0:T(8,128)(2,1)S(1)} %slice.223), channel_id=1, source_target_pairs={{0,32},{32,64},{64,96},{96,128},{128,160},{160,192},{192,224},{1,3... | collective-permute-start | bytes 198152 | tf_op jit(solution)/shard_map/ppermute | solution.py:45
  490.7 76.1 %copy-start.1 = (bf16[512,256]{1,0:T(8,128)(2,1)S(1)}, bf16[512,256]{1,0:T(8,128)(2,1)}, u32[]{:S(2)}) copy-start(bf16[512,256]{1,0:T(8,128)(2,1)} %param.13) | copy-start | bytes 786436
  490.7 68.6 %collective-permute-start.9 = (bf16[192,256]{1,0:T(8,128)(2,1)S(1)}, bf16[192,256]{1,0:T(8,128)(2,1)S(1)}, u32[]{:S(2)}, u32[]{:S(2)}) collective-permute-start(bf16[192,256]{1,0:T(8,128)(2,1)S(1)} %copy-done.5), channel_id=1, source_target_pairs={{128,0},{129,1},{130,2},{131,3},{132,4},{133,5},{134,6},{135,7},{1... | collective-permute-start | bytes 294920 | tf_op jit(solution)/shard_map/ppermute | solution.py:99
  559.3 6.7 %collective-permute-start.8 = (bf16[192,256]{1,0:T(8,128)(2,1)S(1)}, bf16[192,256]{1,0:T(8,128)(2,1)S(1)}, u32[]{:S(2)}, u32[]{:S(2)}) collective-permute-start(bf16[192,256]{1,0:T(8,128)(2,1)S(1)} %get-tuple-element.274), channel_id=1, source_target_pairs={{0,128},{1,129},{2,130},{3,131},{4,132},{5,133},{6,134},{7,135},{8... | collective-permute-start | bytes 294920 | tf_op jit(solution)/shard_map/ppermute | solution.py:100
Sparse Core Ops, SparseCore 0:
  219.4 67.7 all-gather.2
  490.8 66.4 all-gather.4
